TPU v7x, 32 devices: a whole 2x2x4 slice. The times are simulated.
32 devices in a mesh: groups: 2 (over y), freq: 4 (over z), src: 2 (over x), vp: 2 (over core).
Axes of the slice: x: 2, y: 2, z: 4, core: 2. Of those that a mesh axis runs over, the one named last changes fastest.
Arguments:
- focus_direct: bfloat16 [4, 2, 192, 8192], P('freq', None, ('groups', 'vp'), 'src'), parts along dimension 2, may hold values from -6 to 6
- u_factors: bfloat16 [4, 32, 2, 32, 2048], P('freq', 'src'), may hold values from -0.1875 to 0.1875
- v_factors: bfloat16 [4, 8, 2, 32, 8192], P('freq', None, None, None, 'src'), may hold values from -0.375 to 0.375
- tile_ranks: int32 [4, 8, 32], P('freq', None, 'src'), may hold values from 16 to 32
- onset_rec: int32 [192, 2048], P(('groups', 'vp'), 'src'), parts along dimension 0, may hold values from 64 to 191
- onset_src: int32 [192, 8192], P(('groups', 'vp'), 'src'), parts along dimension 0, may hold values from 64 to 191
Outputs:
- focus_plus: bfloat16 [4, 2, 192, 8192], P('freq', None, ('groups', 'vp'), 'src'), parts along dimension 2
- focus_minus: bfloat16 [4, 2, 192, 2048], P('freq', None, ('groups', 'vp'), 'src'), parts along dimension 2
There are 2 independent parts, one for each index of `groups`. A program takes and returns all parts, laid end to end along the dimension named above; an argument that names none is the same for every part. Nothing has to cross between parts.
All inputs are finite; a program needn't handle non-finite values.
Results may differ from a plain program's by a relative error of at most 0.018.
Values may be sent and summed in bfloat16 or wider, within the bound.
No kernel may reach another device: no remote copies, remote signals or barrier semaphores. Data moves between devices by JAX's collectives and lax.ppermute only.
A program may use at most 128 MiB of HBM per device.

v0:
```python
import math
import jax
import jax.numpy as jnp
from jax import lax
from jax.sharding import PartitionSpec as P

TILE = 256
RANK = 32
NT = 256
FLO = 8
ITERS = 2


def make_tables(count):
    index = FLO + jnp.arange(count, dtype=jnp.int32)
    sample = jnp.arange(NT, dtype=jnp.int32)
    phase = (index[:, None] * sample[None, :] % NT).astype(jnp.float32) * (2.0 * math.pi / NT)
    cosine = jnp.cos(phase)
    sine = jnp.sin(phase)
    inverse = jnp.stack([cosine, -sine]) * (2.0 / NT)
    forward = jnp.stack([cosine, -sine])
    return (inverse, forward)


def window(spectrum, onset):
    inverse, forward = make_tables(spectrum.shape[0])
    signal = jnp.einsum("fcvm,cft->vmt", spectrum, inverse, precision=lax.Precision.HIGHEST)
    keep = jnp.arange(NT, dtype=jnp.int32)[None, None, :] < onset[:, :, None]
    signal = jnp.where(keep, signal, jnp.zeros_like(signal))
    return jnp.einsum("vmt,cft->fcvm", signal, forward, precision=lax.Precision.HIGHEST)


def coefficients(v_fac, mask, focus):
    points = focus.shape[1]
    row_tiles = v_fac.shape[0]
    col_tiles = v_fac.shape[-1] // TILE
    source = focus.reshape(2, points, col_tiles, TILE)
    v_tiles = v_fac.reshape(row_tiles, 2, RANK, col_tiles, TILE)
    form = "irjt,vjt->ivjr"
    z_real = jnp.einsum(
        form, v_tiles[:, 0], source[0], preferred_element_type=jnp.float32
    ) + jnp.einsum(form, v_tiles[:, 1], source[1], preferred_element_type=jnp.float32)
    z_imag = jnp.einsum(
        form, v_tiles[:, 0], source[1], preferred_element_type=jnp.float32
    ) - jnp.einsum(form, v_tiles[:, 1], source[0], preferred_element_type=jnp.float32)
    z_real = jnp.where(mask, z_real, 0.0).astype(jnp.bfloat16)
    z_imag = jnp.where(mask, z_imag, 0.0).astype(jnp.bfloat16)
    return jnp.stack([z_real, z_imag])


def expand_rows(u_fac, coeff):
    col_tiles = u_fac.shape[0]
    row_tiles = u_fac.shape[-1] // TILE
    points = coeff.shape[2]
    u_tiles = u_fac.reshape(col_tiles, 2, RANK, row_tiles, TILE)
    other = "jrit,ivjr->vit"
    y_real = jnp.einsum(
        other, u_tiles[:, 0], coeff[0], preferred_element_type=jnp.float32
    ) - jnp.einsum(other, u_tiles[:, 1], coeff[1], preferred_element_type=jnp.float32)
    y_imag = jnp.einsum(
        other, u_tiles[:, 0], coeff[1], preferred_element_type=jnp.float32
    ) + jnp.einsum(other, u_tiles[:, 1], coeff[0], preferred_element_type=jnp.float32)
    return jnp.stack([y_real.reshape(points, -1), y_imag.reshape(points, -1)])


def forward_local(u_fac, v_fac, mask, focus):
    return expand_rows(u_fac, coefficients(v_fac, mask, focus))


def adjoint_local(u_fac, v_fac, mask, focus):
    points = focus.shape[1]
    col_tiles = u_fac.shape[0]
    row_tiles = v_fac.shape[0]
    receiver = focus.reshape(2, points, row_tiles, TILE)
    v_tiles = v_fac.reshape(row_tiles, 2, RANK, col_tiles, TILE)
    u_tiles = u_fac.reshape(col_tiles, 2, RANK, row_tiles, TILE)
    form = "jrit,vit->ivjr"
    w_real = jnp.einsum(
        form, u_tiles[:, 0], receiver[0], preferred_element_type=jnp.float32
    ) + jnp.einsum(form, u_tiles[:, 1], receiver[1], preferred_element_type=jnp.float32)
    w_imag = jnp.einsum(
        form, u_tiles[:, 0], receiver[1], preferred_element_type=jnp.float32
    ) - jnp.einsum(form, u_tiles[:, 1], receiver[0], preferred_element_type=jnp.float32)
    w_real = jnp.where(mask, w_real, 0.0).astype(jnp.bfloat16)
    w_imag = jnp.where(mask, w_imag, 0.0).astype(jnp.bfloat16)
    other = "irjt,ivjr->vjt"
    x_real = jnp.einsum(
        other, v_tiles[:, 0], w_real, preferred_element_type=jnp.float32
    ) - jnp.einsum(other, v_tiles[:, 1], w_imag, preferred_element_type=jnp.float32)
    x_imag = jnp.einsum(
        other, v_tiles[:, 0], w_imag, preferred_element_type=jnp.float32
    ) + jnp.einsum(other, v_tiles[:, 1], w_real, preferred_element_type=jnp.float32)
    return jnp.stack([x_real.reshape(points, -1), x_imag.reshape(points, -1)])


def per_device(focus_direct, u_factors, v_factors, tile_ranks, onset_rec, onset_src):
    freq_count = lax.axis_size("freq")
    rank_index = jnp.arange(RANK, dtype=jnp.int32)
    masks = (rank_index[None, None, None, :] < tile_ranks[:, :, :, None])[:, :, None]
    rec_block = onset_rec.shape[1]
    rec_piece = rec_block // freq_count
    src_piece = onset_src.shape[1] // freq_count
    freq_place = lax.axis_index("freq")
    rec_onset = lax.dynamic_slice_in_dim(onset_rec, freq_place * rec_piece, rec_piece, 1)
    src_onset = lax.dynamic_slice_in_dim(onset_src, freq_place * src_piece, src_piece, 1)
    plus = focus_direct
    minus = None
    for sweep in range(ITERS):
        partial_terms = jax.vmap(forward_local)(u_factors, v_factors, masks, plus)
        summed = lax.psum_scatter(
            partial_terms.astype(jnp.bfloat16), "src", scatter_dimension=3, tiled=True
        ).astype(jnp.float32)
        traces = lax.all_to_all(
            summed.astype(jnp.bfloat16), "freq", split_axis=3, concat_axis=0, tiled=True
        ).astype(summed.dtype)
        windowed = window(traces, rec_onset).astype(jnp.bfloat16)
        minus = lax.all_to_all(windowed, "freq", split_axis=0, concat_axis=3, tiled=True)
        minus_all = lax.all_gather(minus, "src", axis=3, tiled=True)
        adjoint = jax.vmap(adjoint_local)(u_factors, v_factors, masks, minus_all)
        source_traces = lax.all_to_all(
            adjoint.astype(jnp.bfloat16), "freq", split_axis=3, concat_axis=0, tiled=True
        ).astype(adjoint.dtype)
        src_windowed = window(source_traces, src_onset)
        returned = lax.all_to_all(
            src_windowed.astype(jnp.bfloat16), "freq", split_axis=0, concat_axis=3, tiled=True
        ).astype(src_windowed.dtype)
        plus = (focus_direct.astype(jnp.float32) + returned).astype(jnp.bfloat16)
    return (plus, minus)


def solution(mesh):
    placed = (
        P("freq", None, ("groups", "vp"), "src"),
        P("freq", "src", None, None, None),
        P("freq", None, None, None, "src"),
        P("freq", None, "src"),
        P(("groups", "vp"), "src"),
        P(("groups", "vp"), "src"),
    )
    return jax.shard_map(
        per_device,
        mesh=mesh,
        in_specs=placed,
        out_specs=(
            P("freq", None, ("groups", "vp"), "src"),
            P("freq", None, ("groups", "vp"), "src"),
        ),
        check_vma=False,
    )
```

profile of v0, /device:TPU:0, one launch (start us, length us, event | category | flops | bytes accessed | tf_op | source)
XLA Modules:
  0.0 478.2 jit_solution(13236355608998709984)
XLA Ops:
  41.8 15.2 %reduce-scatter.3.cloned.1.call-done = bf16[1,2,48,1024]{3,2,1,0:T(8,128)(2,1)} async-done(((bf16[1,2,48,2048]{3,2,1,0:T(8,128)(2,1)}), bf16[1,2,48,1024]{3,2,1,0:T(8,128)(2,1)}) %reduce-scatter.3.cloned.1.call-update) | async-done | bytes 196624 | tf_op jit(solution)/shard_map/reduce_scatter | solution.py:110
  59.7 4.6 all-to-all-start
  64.4 7.4 %all-to-all-done = bf16[4,2,12288]{2,1,0:T(2,128)(2,1)} async-done(((bf16[4,2,12288]{2,1,0:T(2,128)(2,1)}), bf16[4,2,12288]{2,1,0:T(2,128)(2,1)}, u32[]{:S(2)}, u32[]{:S(2)}) %all-to-all-start) | async-done | bytes 196640 | tf_op jit(solution)/shard_map/all_to_all | solution.py:113
  74.3 6.0 %fusion.168 = f32[48,256,256,1]{2,1,0,3:T(8,128)S(1)} fusion(bf16[1,2,48,4,256]{4,3,2,1,0:T(4,128)(2,1)} %copy.170, f32[1,4,256]{2,1,0:T(4,128)S(1)} %get-tuple-element.27, f32[1,4,256]{2,1,0:T(4,128)S(1)} %get-tuple-element.26), kind=kOutput, calls=%fused_computation.144 | convolution fusion | flops 301993984 | bytes 12787712 | tf_op jit(solution)/shard_map/fcvm,cft->vmt/dot_general | solution.py:27
  80.3 12.0 %fusion.143 = bf16[4,2,48,256]{3,0,2,1:T(4,128)(2,1)S(1)} fusion(f32[48,256,256,1]{2,1,0,3:T(8,128)S(1)} %fusion.168, s32[48,256]{1,0:T(8,128)S(1)} %constant_dynamic-slice_fusion, f32[1,4,256]{2,1,0:T(4,128)S(1)} %get-tuple-element.27, f32[1,4,256]{2,1,0:T(4,128)S(1)} %get-tuple-element.26), kind=kOutput, calls=%fused_computation.109 | convolution fusion | flops 308381696 | bytes 12836864 | tf_op jit(solution)/shard_map/vmt,cft->fcvm/dot_general | solution.py:30
  102.9 6.5 %all_gather.6 = bf16[1,2,48,2048]{3,2,1,0:T(8,128)(2,1)S(1)} all-gather(bf16[1,2,48,1024]{3,2,1,0:T(8,128)(2,1)S(1)} %bitcast.606), channel_id=1, replica_groups=mesh['groups'=2,'freq'=4,'src'=2,'vp'=2] {'src'}, dimensions={3}, use_global_device_ids=true | all-gather | bytes 589824 | tf_op jit(solution)/shard_map/all_gather | solution.py:118
  125.6 5.4 %copy.140 = bf16[1,2,48,4096]{2,1,0,3:T(2,128)(2,1)} copy(bf16[1,2,48,4096]{3,2,1,0:T(8,128)(2,1)} %maximum_bitcast_fusion) | data formatting | bytes 1572864 | tf_op jit(solution)/shard_map/convert_element_type | solution.py:121
  131.1 5.1 %reshape.570 = bf16[4,2,49152]{2,1,0:T(2,128)(2,1)} reshape(bf16[4096,1,2,48]{3,2,1,0:T(2,128)(2,1)} %bitcast.582) | data formatting | bytes 1572864
  140.6 17.3 %all-to-all-done.2 = bf16[4,2,49152]{2,1,0:T(2,128)(2,1)} async-done(((bf16[4,2,49152]{2,1,0:T(2,128)(2,1)}), bf16[4,2,49152]{2,1,0:T(2,128)(2,1)}, u32[]{:S(2)}, u32[]{:S(2)}) %all-to-all-start.2) | async-done | bytes 786464 | tf_op jit(solution)/shard_map/all_to_all | solution.py:120
  157.9 4.9 %reshape.571 = bf16[4096,1,2,48]{3,2,1,0:T(2,128)(2,1)} reshape(bf16[4,2,49152]{2,1,0:T(2,128)(2,1)} %all-to-all-done.2) | data formatting | bytes 1572864
  162.8 5.0 %copy.171 = bf16[1,2,48,4,1024]{4,3,2,1,0:T(4,128)(2,1)S(1)} copy(bf16[1,2,48,4,1024]{2,1,4,3,0:T(2,128)(2,1)} %bitcast.583) | data formatting | bytes 1572864 | tf_op jit(solution)/shard_map/all_to_all | solution.py:120
  167.8 24.2 %fusion.156 = f32[48,1024,256,1]{2,1,0,3:T(8,128)} fusion(bf16[1,2,48,4,1024]{4,3,2,1,0:T(4,128)(2,1)S(1)} %copy.171, f32[1,4,256]{2,1,0:T(4,128)S(1)} %get-tuple-element.27, f32[1,4,256]{2,1,0:T(4,128)S(1)} %get-tuple-element.26), kind=kOutput, calls=%fused_computation.122 | convolution fusion | flops 1207963648 | bytes 51126272 | tf_op jit(solution)/shard_map/fcvm,cft->vmt/dot_general | solution.py:27
  192.1 46.6 %fusion.79 = bf16[4,2,48,1024]{3,0,2,1:T(4,128)(2,1)S(1)} fusion(f32[48,1024,256,1]{2,1,0,3:T(8,128)} %fusion.156, s32[48,1024]{1,0:T(8,128)S(1)} %constant_dynamic-slice_fusion.1, f32[1,4,256]{2,1,0:T(4,128)S(1)} %get-tuple-element.27, f32[1,4,256]{2,1,0:T(4,128)S(1)} %get-tuple-element.26), kind=kOutput, calls=%fused_computation.77 | convolution fusion | flops 1233520640 | bytes 51322880 | tf_op jit(solution)/shard_map/vmt,cft->fcvm/dot_general | solution.py:30
  238.9 20.7 %all_to_all.126 = bf16[4,2,48,1024]{3,2,1,0:T(8,128)(2,1)S(1)} all-to-all(bf16[4,2,48,1024]{3,2,1,0:T(8,128)(2,1)S(1)} %copy.142), channel_id=1, replica_groups=mesh['groups'=2,'freq'=4,'src'=2,'vp'=2] {'freq'}, dimensions={0} | all-to-all | bytes 1572864 | tf_op jit(solution)/shard_map/all_to_all | solution.py:124
  272.6 11.4 %reduce-scatter.5.cloned.1.call-done = bf16[1,2,48,1024]{3,2,1,0:T(8,128)(2,1)} async-done(((bf16[1,2,48,2048]{3,2,1,0:T(8,128)(2,1)}), bf16[1,2,48,1024]{3,2,1,0:T(8,128)(2,1)}) %reduce-scatter.5.cloned.1.call-update) | async-done | bytes 196624 | tf_op jit(solution)/shard_map/reduce_scatter | solution.py:110
  286.0 12.1 %all_to_all.127 = bf16[4,2,12288]{2,1,0:T(2,128)(2,1)S(1)} all-to-all(bf16[4,2,12288]{2,1,0:T(2,128)(2,1)S(1)} %reshape.572), channel_id=1, replica_groups=mesh['groups'=2,'freq'=4,'src'=2,'vp'=2] {'freq'}, dimensions={0} | all-to-all | bytes 393216 | tf_op jit(solution)/shard_map/all_to_all | solution.py:113
  299.1 5.1 %fusion.166 = f32[48,256,256,1]{2,1,0,3:T(8,128)S(1)} fusion(bf16[1,2,48,4,256]{4,3,2,1,0:T(4,128)(2,1)S(1)} %copy.172, f32[1,4,256]{2,1,0:T(4,128)S(1)} %get-tuple-element.27, f32[1,4,256]{2,1,0:T(4,128)S(1)} %get-tuple-element.26), kind=kOutput, calls=%fused_computation.142 | convolution fusion | flops 301993984 | bytes 12787712 | tf_op jit(solution)/shard_map/fcvm,cft->vmt/dot_general | solution.py:27
  304.2 12.0 %fusion.140 = bf16[4,2,48,256]{3,0,2,1:T(4,128)(2,1)S(1)} fusion(f32[48,256,256,1]{2,1,0,3:T(8,128)S(1)} %fusion.166, s32[48,256]{1,0:T(8,128)S(1)} %constant_dynamic-slice_fusion, f32[1,4,256]{2,1,0:T(4,128)S(1)} %get-tuple-element.27, f32[1,4,256]{2,1,0:T(4,128)S(1)} %get-tuple-element.26), kind=kOutput, calls=%fused_computation.108 | convolution fusion | flops 308381696 | bytes 12836864 | tf_op jit(solution)/shard_map/vmt,cft->fcvm/dot_general | solution.py:30
  316.3 10.0 %all_to_all.128 = bf16[4,2,48,256]{3,2,1,0:T(8,128)(2,1)S(1)} all-to-all(bf16[4,2,48,256]{3,2,1,0:T(8,128)(2,1)S(1)} %copy.150), channel_id=1, replica_groups=mesh['groups'=2,'freq'=4,'src'=2,'vp'=2] {'freq'}, dimensions={0} | all-to-all | bytes 393216 | tf_op jit(solution)/shard_map/all_to_all | solution.py:117
  326.3 6.3 %all_gather.7 = bf16[1,2,48,2048]{3,2,1,0:T(8,128)(2,1)S(1)} all-gather(bf16[1,2,48,1024]{3,2,1,0:T(8,128)(2,1)S(1)} %bitcast.604), channel_id=1, replica_groups=mesh['groups'=2,'freq'=4,'src'=2,'vp'=2] {'src'}, dimensions={3}, use_global_device_ids=true | all-gather | bytes 589824 | tf_op jit(solution)/shard_map/all_gather | solution.py:118
  349.0 21.8 %all_to_all.129 = bf16[4,2,49152]{2,1,0:T(2,128)(2,1)} all-to-all(bf16[4,2,49152]{2,1,0:T(2,128)(2,1)S(1)} %reshape.574), channel_id=1, replica_groups=mesh['groups'=2,'freq'=4,'src'=2,'vp'=2] {'freq'}, dimensions={0} | all-to-all | bytes 1572864 | tf_op jit(solution)/shard_map/all_to_all | solution.py:120
  375.9 24.2 %fusion.154 = f32[48,1024,256,1]{2,1,0,3:T(8,128)} fusion(bf16[1,2,48,4,1024]{4,3,2,1,0:T(4,128)(2,1)S(1)} %copy.173, f32[1,4,256]{2,1,0:T(4,128)S(1)} %get-tuple-element.27, f32[1,4,256]{2,1,0:T(4,128)S(1)} %get-tuple-element.26), kind=kOutput, calls=%fused_computation.120 | convolution fusion | flops 1207963648 | bytes 51126272 | tf_op jit(solution)/shard_map/fcvm,cft->vmt/dot_general | solution.py:27
  400.1 46.6 %fusion.76 = bf16[4,2,48,1024]{3,0,2,1:T(4,128)(2,1)S(1)} fusion(f32[48,1024,256,1]{2,1,0,3:T(8,128)} %fusion.154, s32[48,1024]{1,0:T(8,128)S(1)} %constant_dynamic-slice_fusion.1, f32[1,4,256]{2,1,0:T(4,128)S(1)} %get-tuple-element.27, f32[1,4,256]{2,1,0:T(4,128)S(1)} %get-tuple-element.26), kind=kOutput, calls=%fused_computation.76 | convolution fusion | flops 1233520640 | bytes 51322880 | tf_op jit(solution)/shard_map/vmt,cft->fcvm/dot_general | solution.py:30
  447.0 21.5 %all_to_all.130 = bf16[4,2,48,1024]{3,2,1,0:T(8,128)(2,1)S(1)} all-to-all(bf16[4,2,48,1024]{3,2,1,0:T(8,128)(2,1)S(1)} %copy.166), channel_id=1, replica_groups=mesh['groups'=2,'freq'=4,'src'=2,'vp'=2] {'freq'}, dimensions={0} | all-to-all | bytes 1572864 | tf_op jit(solution)/shard_map/all_to_all | solution.py:124
  (160 shorter events, 110.8 us)
Async XLA Ops:
  7.2 133.4 %copy-start = (s32[48,4096]{1,0:T(8,128)S(1)}, s32[48,4096]{1,0:T(8,128)}, u32[]{:S(2)}) copy-start(s32[48,4096]{1,0:T(8,128)} %param.11) | copy-start | bytes 2359300
  7.2 49.7 %reduce-scatter.3.cloned.1.call-start = ((), (), s32[]{:S(2)}) async-start(), calls=%async_computation.10 | async-start | bytes 589824 | tf_op jit(solution)/shard_map/reduce_scatter | solution.py:110
  16.3 2.1 copy-start.2
  21.2 2.1 copy-start.4
  23.3 2.1 copy-start.24
  29.2 3.2 copy-start.16
  29.2 3.2 copy-start.17
  29.2 4.8 copy-start.18
  29.2 5.7 %copy-start.19 = (f32[16,48,256]{1,2,0:S(1)}, f32[16,48,256]{1,2,0}, u32[]{:S(2)}) copy-start(f32[16,48,256]{1,2,0} %fusion.161) | copy-start | bytes 2359300
  32.4 4.8 %copy-start.6 = (bf16[1,16,1,32,8,256]{5,4,3,2,1,0:T(8,128)(2,1)}, bf16[1,16,1,32,8,256]{5,4,3,2,1,0:T(8,128)(2,1)S(1)}, u32[]{:S(2)}) copy-start(bf16[1,16,1,32,8,256]{5,4,3,2,1,0:T(8,128)(2,1)S(1)} %get-tuple-element.9) | copy-start | bytes 6291460
  59.7 12.2 %all-to-all-start = ((bf16[4,2,12288]{2,1,0:T(2,128)(2,1)}), bf16[4,2,12288]{2,1,0:T(2,128)(2,1)}, u32[]{:S(2)}, u32[]{:S(2)}) async-start(bf16[4,2,12288]{2,1,0:T(2,128)(2,1)} %reshape.568), calls=%async_computation.1 | async-start | bytes 393216 | tf_op jit(solution)/shard_map/all_to_all | solution.py:113
  93.1 9.8 %all-to-all-start.1 = ((bf16[4,2,48,256]{3,2,1,0:T(8,128)(2,1)}), bf16[4,2,48,256]{3,2,1,0:T(8,128)(2,1)S(1)}, u32[]{:S(2)}, u32[]{:S(2)}) async-start(bf16[4,2,48,256]{3,2,1,0:T(8,128)(2,1)} %copy.126), calls=%async_computation.2 | async-start | bytes 393216 | tf_op jit(solution)/shard_map/all_to_all | solution.py:117
  96.7 3.6 copy-start.20
  102.9 6.6 %copy-start.8 = (bf16[16,32,8,256]{3,1,0,2:T(8,128)(2,1)S(1)}, bf16[16,32,8,256]{3,1,0,2:T(8,128)(2,1)}, u32[]{:S(2)}) copy-start(bf16[16,32,8,256]{3,1,0,2:T(8,128)(2,1)} %copy.131) | copy-start | bytes 6291460
  113.2 1.6 copy-start.14
  115.6 1.6 copy-start.12
  136.2 21.7 %all-to-all-start.2 = ((bf16[4,2,49152]{2,1,0:T(2,128)(2,1)}), bf16[4,2,49152]{2,1,0:T(2,128)(2,1)}, u32[]{:S(2)}, u32[]{:S(2)}) async-start(bf16[4,2,49152]{2,1,0:T(2,128)(2,1)} %reshape.570), calls=%async_computation.3 | async-start | bytes 1572864 | tf_op jit(solution)/shard_map/all_to_all | solution.py:120
  140.6 143.4 %reduce-scatter.5.cloned.1.call-start = ((), (), s32[]{:S(2)}) async-start(), calls=%async_computation.11 | async-start | bytes 589824 | tf_op jit(solution)/shard_map/reduce_scatter | solution.py:110
  266.4 1.6 copy-start.7
  316.2 16.6 %copy-start.9 = (bf16[16,32,8,256]{3,1,0,2:T(8,128)(2,1)S(1)}, bf16[16,32,8,256]{3,1,0,2:T(8,128)(2,1)}, u32[]{:S(2)}) copy-start(bf16[16,32,8,256]{3,1,0,2:T(8,128)(2,1)} %copy.131) | copy-start | bytes 6291460
  326.3 6.4 %copy-start.23 = (bf16[1,4,2,6,8,256]{5,4,1,3,2,0:T(8,128)(2,1)}, bf16[1,4,2,6,8,256]{5,4,1,3,2,0:T(8,128)(2,1)S(1)}, u32[]{:S(2)}) copy-start(bf16[1,4,2,6,8,256]{5,4,1,3,2,0:T(8,128)(2,1)S(1)} %copy.192) | copy-start | bytes 589828
  336.5 1.6 copy-start.15
  338.9 1.6 copy-start.13
  468.7 2.2 copy-start.1
  (6 other events, 8.6 us)
Sparse Core Ops, SparseCore 0:
  41.1 15.7 reduce-scatter.2
  272.7 11.1 reduce-scatter.4
where the time goes:
time: 486 us; the launch traced here: 478 us
  matrix products  207 us (43%)
  blocking collectives  99 us (20%)
  local copies, waits for them, and re-layouts  81.7 us (17%)
  waiting for transfers between devices  52 us (11%)
  between operations  15.2 us (3%)
  starting transfers between devices  12.6 us (3%)
  other arithmetic  10.8 us (2%)
    dot_general x4, matrix products, window(): jnp.einsum('vmt,cft->fcvm', signal, forward, precision=lax.Precision.HIGH...  117 us
    dot_general x4, matrix products, window(): jnp.einsum('fcvm,cft->vmt', spectrum, inverse, precision=lax.Precision.HI...  59.6 us
    unnamed x66, local copies, waits for them, and re-layouts  42.3 us
    all_to_all x2, blocking collectives, per_device(): lax.all_to_all(src_windowed.astype(jnp.bfloat16), 'freq', split_axis=0, c...  42.2 us
    reduce_scatter x2, waiting for transfers between devices, per_device(): lax.psum_scatter(partial_terms.astype(jnp.bfloat16), 'src', scatter_dimen...  26.5 us
    all_to_all x1, blocking collectives, per_device(): lax.all_to_all(adjoint.astype(jnp.bfloat16), 'freq', split_axis=3, concat...  21.8 us
    all_to_all x1, waiting for transfers between devices, per_device(): lax.all_to_all(adjoint.astype(jnp.bfloat16), 'freq', split_axis=3, concat...  17.3 us
    unnamed x16, matrix products  16.6 us
  transfers between devices with their start and end apart: 5, of which 5 were waited for; matrix products, arithmetic and copies ran while one was open for 1% of the time, Pallas kernels for 0%

commit v1 on v0

--- a/solution.py
+++ b/solution.py
@@ -121,8 +121,16 @@
             adjoint.astype(jnp.bfloat16), "freq", split_axis=3, concat_axis=0, tiled=True
         ).astype(adjoint.dtype)
         src_windowed = window(source_traces, src_onset)
-        returned = lax.all_to_all(
-            src_windowed.astype(jnp.bfloat16), "freq", split_axis=0, concat_axis=3, tiled=True
+        returned = jnp.concatenate(
+            lax.all_to_all(
+                jnp.stack(
+                    jnp.split(src_windowed.astype(jnp.bfloat16), lax.axis_size("freq"), axis=0)
+                ),
+                "freq",
+                0,
+                0,
+            ),
+            axis=3,
         ).astype(src_windowed.dtype)
         plus = (focus_direct.astype(jnp.float32) + returned).astype(jnp.bfloat16)
     return (plus, minus)

time: 486 us -> 489 us (level)
    unnamed x66 -> x72, local copies, waits for them, and re-layouts: 42.3 us -> 42.7 us
where the time goes in v1:
time: 489 us; the launch traced here: 481 us
  matrix products  207 us (42%)
  blocking collectives  99.5 us (20%)
  local copies, waits for them, and re-layouts  83.9 us (17%)
  waiting for transfers between devices  52 us (11%)
  between operations  15.1 us (3%)
  starting transfers between devices  12.6 us (3%)
  other arithmetic  11.2 us (2%)
    dot_general x4, matrix products, window(): jnp.einsum('vmt,cft->fcvm', signal, forward, precision=lax.Precision.HIGH...  117 us
    dot_general x4, matrix products, window(): jnp.einsum('fcvm,cft->vmt', spectrum, inverse, precision=lax.Precision.HI...  59.5 us
    unnamed x72, local copies, waits for them, and re-layouts  42.7 us
    all_to_all x2, blocking collectives, per_device(): lax.all_to_all(jnp.stack(jnp.split(src_windowed.astype(jnp.bfloat16), lax...  42.3 us
    reduce_scatter x2, waiting for transfers between devices, per_device(): lax.psum_scatter(partial_terms.astype(jnp.bfloat16), 'src', scatter_dimen...  26.5 us
    all_to_all x1, blocking collectives, per_device(): lax.all_to_all(adjoint.astype(jnp.bfloat16), 'freq', split_axis=3, concat...  22 us
    all_to_all x1, waiting for transfers between devices, per_device(): lax.all_to_all(adjoint.astype(jnp.bfloat16), 'freq', split_axis=3, concat...  17.2 us
    unnamed x16, matrix products  16.5 us
  transfers between devices with their start and end apart: 5, of which 5 were waited for; matrix products, arithmetic and copies ran while one was open for 1% of the time, Pallas kernels for 0%

profile of v1, /device:TPU:0, one launch (start us, length us, event | category | flops | bytes accessed | tf_op | source)
XLA Modules:
  0.0 481.0 jit_solution(3658555383796290127)
XLA Ops:
  42.0 15.2 %reduce-scatter.3.cloned.1.call-done = bf16[1,2,48,1024]{3,2,1,0:T(8,128)(2,1)} async-done(((bf16[1,2,48,2048]{3,2,1,0:T(8,128)(2,1)}), bf16[1,2,48,1024]{3,2,1,0:T(8,128)(2,1)}) %reduce-scatter.3.cloned.1.call-update) | async-done | bytes 196624 | tf_op jit(solution)/shard_map/reduce_scatter | solution.py:110
  59.9 4.6 all-to-all-start
  64.6 7.5 %all-to-all-done = bf16[4,2,12288]{2,1,0:T(2,128)(2,1)} async-done(((bf16[4,2,12288]{2,1,0:T(2,128)(2,1)}), bf16[4,2,12288]{2,1,0:T(2,128)(2,1)}, u32[]{:S(2)}, u32[]{:S(2)}) %all-to-all-start) | async-done | bytes 196640 | tf_op jit(solution)/shard_map/all_to_all | solution.py:113
  74.6 6.0 %fusion.168 = f32[48,256,256,1]{2,1,0,3:T(8,128)S(1)} fusion(bf16[1,2,48,4,256]{4,3,2,1,0:T(4,128)(2,1)} %copy.302, f32[1,4,256]{2,1,0:T(4,128)S(1)} %get-tuple-element.35, f32[1,4,256]{2,1,0:T(4,128)S(1)} %get-tuple-element.34), kind=kOutput, calls=%fused_computation.154 | convolution fusion | flops 301993984 | bytes 12787712 | tf_op jit(solution)/shard_map/fcvm,cft->vmt/dot_general | solution.py:27
  80.6 12.0 %fusion.143 = bf16[4,2,48,256]{3,0,2,1:T(4,128)(2,1)S(1)} fusion(f32[48,256,256,1]{2,1,0,3:T(8,128)S(1)} %fusion.168, s32[48,256]{1,0:T(8,128)S(1)} %constant_dynamic-slice_fusion, f32[1,4,256]{2,1,0:T(4,128)S(1)} %get-tuple-element.35, f32[1,4,256]{2,1,0:T(4,128)S(1)} %get-tuple-element.34), kind=kOutput, calls=%fused_computation.109 | convolution fusion | flops 308381696 | bytes 12836864 | tf_op jit(solution)/shard_map/vmt,cft->fcvm/dot_general | solution.py:30
  103.1 6.5 %all_gather.6 = bf16[1,2,48,2048]{3,2,1,0:T(8,128)(2,1)S(1)} all-gather(bf16[1,2,48,1024]{3,2,1,0:T(8,128)(2,1)S(1)} %bitcast.624), channel_id=1, replica_groups=mesh['groups'=2,'freq'=4,'src'=2,'vp'=2] {'src'}, dimensions={3}, use_global_device_ids=true | all-gather | bytes 589824 | tf_op jit(solution)/shard_map/all_gather | solution.py:118
  125.9 5.4 %copy.274 = bf16[1,2,48,4096]{2,1,0,3:T(2,128)(2,1)} copy(bf16[1,2,48,4096]{3,2,1,0:T(8,128)(2,1)} %maximum_bitcast_fusion) | data formatting | bytes 1572864 | tf_op jit(solution)/shard_map/convert_element_type | solution.py:121
  131.3 5.1 %reshape.568 = bf16[4,2,49152]{2,1,0:T(2,128)(2,1)} reshape(bf16[4096,1,2,48]{3,2,1,0:T(2,128)(2,1)} %bitcast.596) | data formatting | bytes 1572864
  140.8 17.2 %all-to-all-done.2 = bf16[4,2,49152]{2,1,0:T(2,128)(2,1)} async-done(((bf16[4,2,49152]{2,1,0:T(2,128)(2,1)}), bf16[4,2,49152]{2,1,0:T(2,128)(2,1)}, u32[]{:S(2)}, u32[]{:S(2)}) %all-to-all-start.2) | async-done | bytes 786464 | tf_op jit(solution)/shard_map/all_to_all | solution.py:120
  158.1 4.7 reshape.569
  162.7 5.0 %copy.303 = bf16[1,2,48,4,1024]{4,3,2,1,0:T(4,128)(2,1)S(1)} copy(bf16[1,2,48,4,1024]{2,1,4,3,0:T(2,128)(2,1)} %bitcast.597) | data formatting | bytes 1572864 | tf_op jit(solution)/shard_map/all_to_all | solution.py:120
  167.8 24.2 %fusion.156 = f32[48,1024,256,1]{2,1,0,3:T(8,128)} fusion(bf16[1,2,48,4,1024]{4,3,2,1,0:T(4,128)(2,1)S(1)} %copy.303, f32[1,4,256]{2,1,0:T(4,128)S(1)} %get-tuple-element.35, f32[1,4,256]{2,1,0:T(4,128)S(1)} %get-tuple-element.34), kind=kOutput, calls=%fused_computation.124 | convolution fusion | flops 1207963648 | bytes 51126272 | tf_op jit(solution)/shard_map/fcvm,cft->vmt/dot_general | solution.py:27
  192.0 46.6 %fusion.79 = bf16[4,2,48,1024]{3,0,2,1:T(4,128)(2,1)S(1)} fusion(f32[48,1024,256,1]{2,1,0,3:T(8,128)} %fusion.156, s32[48,1024]{1,0:T(8,128)S(1)} %constant_dynamic-slice_fusion.1, f32[1,4,256]{2,1,0:T(4,128)S(1)} %get-tuple-element.35, f32[1,4,256]{2,1,0:T(4,128)S(1)} %get-tuple-element.34), kind=kOutput, calls=%fused_computation.77 | convolution fusion | flops 1233520640 | bytes 51322880 | tf_op jit(solution)/shard_map/vmt,cft->fcvm/dot_general | solution.py:30
  240.2 20.7 %all_to_all.118 = bf16[4,1,2,48,1024]{4,3,2,1,0:T(8,128)(2,1)S(1)} all-to-all(bf16[4,1,2,48,1024]{4,3,2,1,0:T(8,128)(2,1)S(1)} %pad_maximum_fusion), channel_id=1, replica_groups=mesh['groups'=2,'freq'=4,'src'=2,'vp'=2] {'freq'}, dimensions={0} | all-to-all | bytes 1572864 | tf_op jit(solution)/shard_map/all_to_all | solution.py:125
  273.9 11.4 %reduce-scatter.5.cloned.1.call-done = bf16[1,2,48,1024]{3,2,1,0:T(8,128)(2,1)} async-done(((bf16[1,2,48,2048]{3,2,1,0:T(8,128)(2,1)}), bf16[1,2,48,1024]{3,2,1,0:T(8,128)(2,1)}) %reduce-scatter.5.cloned.1.call-update) | async-done | bytes 196624 | tf_op jit(solution)/shard_map/reduce_scatter | solution.py:110
  287.3 12.3 %all_to_all.119 = bf16[4,2,12288]{2,1,0:T(2,128)(2,1)S(1)} all-to-all(bf16[4,2,12288]{2,1,0:T(2,128)(2,1)S(1)} %reshape.570), channel_id=1, replica_groups=mesh['groups'=2,'freq'=4,'src'=2,'vp'=2] {'freq'}, dimensions={0} | all-to-all | bytes 393216 | tf_op jit(solution)/shard_map/all_to_all | solution.py:113
  300.6 5.1 %fusion.166 = f32[48,256,256,1]{2,1,0,3:T(8,128)S(1)} fusion(bf16[1,2,48,4,256]{4,3,2,1,0:T(4,128)(2,1)S(1)} %copy.304, f32[1,4,256]{2,1,0:T(4,128)S(1)} %get-tuple-element.35, f32[1,4,256]{2,1,0:T(4,128)S(1)} %get-tuple-element.34), kind=kOutput, calls=%fused_computation.152 | convolution fusion | flops 301993984 | bytes 12787712 | tf_op jit(solution)/shard_map/fcvm,cft->vmt/dot_general | solution.py:27
  305.7 12.0 %fusion.140 = bf16[4,2,48,256]{3,0,2,1:T(4,128)(2,1)S(1)} fusion(f32[48,256,256,1]{2,1,0,3:T(8,128)S(1)} %fusion.166, s32[48,256]{1,0:T(8,128)S(1)} %constant_dynamic-slice_fusion, f32[1,4,256]{2,1,0:T(4,128)S(1)} %get-tuple-element.35, f32[1,4,256]{2,1,0:T(4,128)S(1)} %get-tuple-element.34), kind=kOutput, calls=%fused_computation.108 | convolution fusion | flops 308381696 | bytes 12836864 | tf_op jit(solution)/shard_map/vmt,cft->fcvm/dot_general | solution.py:30
  317.8 10.0 %all_to_all.120 = bf16[4,2,48,256]{3,2,1,0:T(8,128)(2,1)S(1)} all-to-all(bf16[4,2,48,256]{3,2,1,0:T(8,128)(2,1)S(1)} %copy.283), channel_id=1, replica_groups=mesh['groups'=2,'freq'=4,'src'=2,'vp'=2] {'freq'}, dimensions={0} | all-to-all | bytes 393216 | tf_op jit(solution)/shard_map/all_to_all | solution.py:117
  327.9 6.3 %all_gather.7 = bf16[1,2,48,2048]{3,2,1,0:T(8,128)(2,1)S(1)} all-gather(bf16[1,2,48,1024]{3,2,1,0:T(8,128)(2,1)S(1)} %bitcast.622), channel_id=1, replica_groups=mesh['groups'=2,'freq'=4,'src'=2,'vp'=2] {'src'}, dimensions={3}, use_global_device_ids=true | all-gather | bytes 589824 | tf_op jit(solution)/shard_map/all_gather | solution.py:118
  350.5 22.0 %all_to_all.121 = bf16[4,2,49152]{2,1,0:T(2,128)(2,1)} all-to-all(bf16[4,2,49152]{2,1,0:T(2,128)(2,1)S(1)} %reshape.572), channel_id=1, replica_groups=mesh['groups'=2,'freq'=4,'src'=2,'vp'=2] {'freq'}, dimensions={0} | all-to-all | bytes 1572864 | tf_op jit(solution)/shard_map/all_to_all | solution.py:120
  377.6 24.2 %fusion.154 = f32[48,1024,256,1]{2,1,0,3:T(8,128)} fusion(bf16[1,2,48,4,1024]{4,3,2,1,0:T(4,128)(2,1)S(1)} %copy.305, f32[1,4,256]{2,1,0:T(4,128)S(1)} %get-tuple-element.35, f32[1,4,256]{2,1,0:T(4,128)S(1)} %get-tuple-element.34), kind=kOutput, calls=%fused_computation.122 | convolution fusion | flops 1207963648 | bytes 51126272 | tf_op jit(solution)/shard_map/fcvm,cft->vmt/dot_general | solution.py:27
  401.8 46.6 %fusion.76 = bf16[4,2,48,1024]{3,0,2,1:T(4,128)(2,1)S(1)} fusion(f32[48,1024,256,1]{2,1,0,3:T(8,128)} %fusion.154, s32[48,1024]{1,0:T(8,128)S(1)} %constant_dynamic-slice_fusion.1, f32[1,4,256]{2,1,0:T(4,128)S(1)} %get-tuple-element.35, f32[1,4,256]{2,1,0:T(4,128)S(1)} %get-tuple-element.34), kind=kOutput, calls=%fused_computation.76 | convolution fusion | flops 1233520640 | bytes 51322880 | tf_op jit(solution)/shard_map/vmt,cft->fcvm/dot_general | solution.py:30
  450.0 21.5 %all_to_all.122 = bf16[4,1,2,48,1024]{4,3,2,1,0:T(8,128)(2,1)S(1)} all-to-all(bf16[4,1,2,48,1024]{4,3,2,1,0:T(8,128)(2,1)S(1)} %pad_maximum_fusion.1), channel_id=1, replica_groups=mesh['groups'=2,'freq'=4,'src'=2,'vp'=2] {'freq'}, dimensions={0} | all-to-all | bytes 1572864 | tf_op jit(solution)/shard_map/all_to_all | solution.py:125
  (168 shorter events, 113.5 us)
Async XLA Ops:
  7.2 133.7 %copy-start = (s32[48,4096]{1,0:T(8,128)S(1)}, s32[48,4096]{1,0:T(8,128)}, u32[]{:S(2)}) copy-start(s32[48,4096]{1,0:T(8,128)} %param.11) | copy-start | bytes 2359300
  7.2 50.0 %reduce-scatter.3.cloned.1.call-start = ((), (), s32[]{:S(2)}) async-start(), calls=%async_computation.10 | async-start | bytes 589824 | tf_op jit(solution)/shard_map/reduce_scatter | solution.py:110
  16.3 2.1 copy-start.2
  21.2 2.0 copy-start.4
  23.2 2.1 copy-start.24
  29.2 3.2 copy-start.16
  29.2 3.2 copy-start.17
  29.2 4.8 copy-start.18
  29.2 5.7 %copy-start.19 = (f32[16,48,256]{1,2,0:S(1)}, f32[16,48,256]{1,2,0}, u32[]{:S(2)}) copy-start(f32[16,48,256]{1,2,0} %fusion.161) | copy-start | bytes 2359300
  32.4 5.1 %copy-start.6 = (bf16[1,16,1,32,8,256]{5,4,3,2,1,0:T(8,128)(2,1)}, bf16[1,16,1,32,8,256]{5,4,3,2,1,0:T(8,128)(2,1)S(1)}, u32[]{:S(2)}) copy-start(bf16[1,16,1,32,8,256]{5,4,3,2,1,0:T(8,128)(2,1)S(1)} %get-tuple-element.9) | copy-start | bytes 6291460
  59.9 12.2 %all-to-all-start = ((bf16[4,2,12288]{2,1,0:T(2,128)(2,1)}), bf16[4,2,12288]{2,1,0:T(2,128)(2,1)}, u32[]{:S(2)}, u32[]{:S(2)}) async-start(bf16[4,2,12288]{2,1,0:T(2,128)(2,1)} %reshape.566), calls=%async_computation.1 | async-start | bytes 393216 | tf_op jit(solution)/shard_map/all_to_all | solution.py:113
  93.4 9.7 %all-to-all-start.1 = ((bf16[4,2,48,256]{3,2,1,0:T(8,128)(2,1)}), bf16[4,2,48,256]{3,2,1,0:T(8,128)(2,1)S(1)}, u32[]{:S(2)}, u32[]{:S(2)}) async-start(bf16[4,2,48,256]{3,2,1,0:T(8,128)(2,1)} %copy.260), calls=%async_computation.2 | async-start | bytes 393216 | tf_op jit(solution)/shard_map/all_to_all | solution.py:117
  96.9 3.6 copy-start.20
  103.1 6.6 %copy-start.8 = (bf16[16,32,8,256]{3,1,0,2:T(8,128)(2,1)S(1)}, bf16[16,32,8,256]{3,1,0,2:T(8,128)(2,1)}, u32[]{:S(2)}) copy-start(bf16[16,32,8,256]{3,1,0,2:T(8,128)(2,1)} %copy.265) | copy-start | bytes 6291460
  113.4 1.6 copy-start.14
  115.8 1.6 copy-start.12
  136.4 21.6 %all-to-all-start.2 = ((bf16[4,2,49152]{2,1,0:T(2,128)(2,1)}), bf16[4,2,49152]{2,1,0:T(2,128)(2,1)}, u32[]{:S(2)}, u32[]{:S(2)}) async-start(bf16[4,2,49152]{2,1,0:T(2,128)(2,1)} %reshape.568), calls=%async_computation.3 | async-start | bytes 1572864 | tf_op jit(solution)/shard_map/all_to_all | solution.py:120
  140.8 144.4 %reduce-scatter.5.cloned.1.call-start = ((), (), s32[]{:S(2)}) async-start(), calls=%async_computation.11 | async-start | bytes 589824 | tf_op jit(solution)/shard_map/reduce_scatter | solution.py:110
  267.7 1.6 copy-start.7
  317.8 16.6 %copy-start.9 = (bf16[16,32,8,256]{3,1,0,2:T(8,128)(2,1)S(1)}, bf16[16,32,8,256]{3,1,0,2:T(8,128)(2,1)}, u32[]{:S(2)}) copy-start(bf16[16,32,8,256]{3,1,0,2:T(8,128)(2,1)} %copy.265) | copy-start | bytes 6291460
  327.9 6.4 %copy-start.23 = (bf16[1,4,2,6,8,256]{5,4,1,3,2,0:T(8,128)(2,1)}, bf16[1,4,2,6,8,256]{5,4,1,3,2,0:T(8,128)(2,1)S(1)}, u32[]{:S(2)}) copy-start(bf16[1,4,2,6,8,256]{5,4,1,3,2,0:T(8,128)(2,1)S(1)} %copy.332) | copy-start | bytes 589828
  338.0 1.6 copy-start.15
  340.4 1.6 copy-start.13
  471.8 2.2 copy-start.1
  (6 other events, 8.6 us)
Sparse Core Ops, SparseCore 0:
  41.3 15.7 reduce-scatter.2
  274.0 11.1 reduce-scatter.4
